TPU v7x, 128 devices: a whole 4x4x4 slice. The times are simulated.
128 devices in a mesh: fsdp: 16 (over z, x_lo, core), seq: 8 (over x_hi, y).
Axes of the slice: x: 4 (x_hi: 2, x_lo: 2; x = x_hi * 2 + x_lo), y: 4, z: 4, core: 2. Of those that a mesh axis runs over, the one named last changes fastest.
Arguments:
- hidden_in: bfloat16 [64, 5, 1536], P('fsdp'), may hold values from -6 to 6
- norm_gain: float32 [1536], replicated, may hold values from 0.1 to 1.9
- w_qkv: bfloat16 [1536, 3, 24, 64], P(None, None, 'seq', 'fsdp'), may hold values from -0.15625 to 0.15625
- w_forget: bfloat16 [1536, 24], replicated, may hold values from -0.15625 to 0.15625
- forget_bias: float32 [24], replicated, may hold values from 1 to 5
- cache_keys: bfloat16 [64, 4096, 1536], P('fsdp', 'seq')
- cache_values: bfloat16 [64, 4096, 1536], P('fsdp', 'seq'), may hold values from -6 to 6
- cache_forget: float32 [64, 24, 4096], P('fsdp', None, 'seq')
- cache_lengths: int32 [64], P('fsdp'), may hold values from 128 to 4096, as said below
- piece_map: int32 [64, 8], P('fsdp'), may hold values from 0 to 7, each once within a row
- draft_counts: int32 [64], P('fsdp'), may hold values from 1 to 4
Outputs:
- verified: bfloat16 [64, 5, 1536], P('fsdp', None, 'seq')
Inputs may be any that keep to these rules, and one draw needn't show every extreme that they name: `cache_lengths`: 16 requests drawn at random have lengths from 3841 to 4096, one exactly 4096; the others have lengths from 128 to 256, one exactly 128.
All inputs are finite; a program needn't handle non-finite values.
Results may differ from a plain program's by a relative error of at most 0.012.
The roundings to bfloat16 on the way count: a program that leaves them out, or rounds other values in their place, can miss the bound.
Values may be sent and summed in bfloat16 or wider, within the bound.
No kernel may reach another device: no remote copies, remote signals or barrier semaphores. Data moves between devices by JAX's collectives and lax.ppermute only.
A program may use at most 128 MiB of HBM per device.

v0:
```python
import jax
import jax.numpy as jnp
from jax import lax
from jax.sharding import PartitionSpec as P

HEAD_DIM = 64
norm_eps = 1e-06
neg_fill = -1e30


def normalize(rows, gain):
    values = rows.astype(jnp.float32)
    mean_sq = jnp.mean(values * values, axis=-1, keepdims=True)
    return (values * lax.rsqrt(mean_sq + norm_eps) * gain).astype(jnp.bfloat16)


def fold_parts(parts):
    maxima, sums, accums = parts
    joint = jnp.max(maxima, axis=0)
    factor = jnp.exp(maxima - joint[None])
    return (joint, jnp.sum(sums * factor, axis=0), jnp.sum(accums * factor[..., None], axis=0))


def body(
    hidden_in,
    norm_gain,
    w_qkv,
    w_forget,
    forget_bias,
    cache_keys,
    cache_values,
    cache_forget,
    cache_lengths,
    piece_map,
    draft_counts,
):
    req_count, new_count, width = hidden_in.shape
    head_count = w_forget.shape[1]
    seq_count = lax.axis_size("seq")
    own_heads = w_qkv.shape[2]
    own_width = own_heads * HEAD_DIM
    piece_len = cache_forget.shape[2]
    logit_scale = HEAD_DIM ** (-0.5)
    seq_index = lax.axis_index("seq")
    head_start = seq_index * own_heads
    normed = normalize(hidden_in, norm_gain).reshape(req_count * new_count, width)
    gate_logit = (
        jnp.dot(normed, w_forget, preferred_element_type=jnp.float32).reshape(
            req_count, new_count, head_count
        )
        + forget_bias
    )
    prefix = jnp.cumsum(jax.nn.log_sigmoid(gate_logit), axis=1)
    projected = jnp.einsum(
        "nd,dchk->nchk",
        normed,
        lax.all_gather(w_qkv, "fsdp", axis=3, tiled=True),
        preferred_element_type=jnp.float32,
    ).astype(jnp.bfloat16)
    own_part = projected.reshape(req_count * new_count, 3, own_width)
    all_heads = lax.all_gather(own_part, "seq", axis=2, tiled=True).reshape(
        req_count, new_count, 3, head_count, HEAD_DIM
    )
    query_rows_all = all_heads[:, :, 0]
    slot_ids = jnp.arange(seq_count, dtype=jnp.int32)
    holders = piece_map[:, :, None] == slot_ids[None, None, :]
    piece_of_slot = jnp.sum(jnp.where(holders, slot_ids[None, :, None], 0), axis=1)
    own_piece = jnp.sum(jnp.where(piece_map == seq_index, slot_ids[None, :], 0), axis=1)
    positions = own_piece[:, None] * piece_len + jnp.arange(piece_len, dtype=jnp.int32)[None, :]
    live_mask = positions < cache_lengths[:, None]
    masked = jnp.where(live_mask[:, None, :], cache_forget, 0.0)
    piece_total = jnp.sum(masked, axis=-1)
    all_totals = lax.all_gather(piece_total[None], "seq", axis=0, tiled=True)
    later_piece = (piece_of_slot.T > own_piece[None, :])[:, :, None]
    later_sum = jnp.sum(jnp.where(later_piece, all_totals, 0.0), axis=0)
    trailing_part = piece_total[..., None] - jnp.cumsum(masked, axis=-1) + later_sum[..., None]
    key_rows = cache_keys.reshape(req_count, piece_len, head_count, HEAD_DIM)
    value_rows = cache_values.reshape(req_count, piece_len, head_count, HEAD_DIM)
    prefix_transposed = jnp.transpose(prefix, (0, 2, 1))
    scores = (
        jnp.einsum("rmhd,rthd->rhmt", query_rows_all, key_rows, preferred_element_type=jnp.float32)
        * logit_scale
    )
    scores = scores + trailing_part[:, :, None, :] + prefix_transposed[..., None]
    key_live = live_mask[:, None, None, :]
    row_max = jnp.max(jnp.where(key_live, scores, neg_fill), axis=-1)
    attn_weights = jnp.where(key_live, jnp.exp(scores - row_max[..., None]), 0.0)
    weight_sum = jnp.sum(attn_weights, axis=-1)
    accum = jnp.einsum(
        "rhmt,rthd->rhmd",
        attn_weights.astype(jnp.bfloat16),
        value_rows,
        preferred_element_type=jnp.float32,
    )
    gathered = (
        lax.all_gather(row_max[None], "seq", axis=0, tiled=True),
        lax.all_gather(weight_sum[None], "seq", axis=0, tiled=True),
        lax.all_gather(accum[None], "seq", axis=0, tiled=True),
    )
    own_parts = tuple(
        (lax.dynamic_slice_in_dim(member, head_start, own_heads, 2) for member in gathered)
    )
    cache_max, cache_sum, cache_acc = fold_parts(own_parts)
    own_rows = own_part.reshape(req_count, new_count, 3, own_heads, HEAD_DIM)
    own_prefix = jnp.transpose(
        lax.dynamic_slice_in_dim(prefix, head_start, own_heads, 2), (0, 2, 1)
    )
    fresh_logits = (
        jnp.einsum(
            "rmhd,rnhd->rhmn",
            own_rows[:, :, 0],
            own_rows[:, :, 1],
            preferred_element_type=jnp.float32,
        )
        * logit_scale
    )
    fresh_logits = fresh_logits + own_prefix[..., :, None] - own_prefix[..., None, :]
    step_ids = jnp.arange(new_count, dtype=jnp.int32)
    causal = (step_ids[None, :] <= step_ids[:, None])[None, None]
    joint_max = jnp.maximum(cache_max, jnp.max(jnp.where(causal, fresh_logits, neg_fill), axis=-1))
    new_weights = jnp.where(causal, jnp.exp(fresh_logits - joint_max[..., None]), 0.0)
    carried = jnp.exp(cache_max - joint_max)
    total_sum = cache_sum * carried + jnp.sum(new_weights, axis=-1)
    blend_weights = cache_acc * carried[..., None] + jnp.einsum(
        "rhmn,rnhd->rhmd",
        new_weights.astype(jnp.bfloat16),
        own_rows[:, :, 2],
        preferred_element_type=jnp.float32,
    )
    result = blend_weights / total_sum[..., None]
    live_rows = (step_ids[None, :] <= draft_counts[:, None])[:, None, :, None]
    result = jnp.where(live_rows, result, 0.0)
    return (
        jnp.transpose(result, (0, 2, 1, 3))
        .reshape(req_count, new_count, own_heads * HEAD_DIM)
        .astype(jnp.bfloat16)
    )


def solution(mesh):
    in_specs = (
        P("fsdp", None, None),
        P(),
        P(None, None, "seq", "fsdp"),
        P(),
        P(),
        P("fsdp", "seq", None),
        P("fsdp", "seq", None),
        P("fsdp", None, "seq"),
        P("fsdp"),
        P("fsdp", None),
        P("fsdp"),
    )
    out_specs = P("fsdp", None, "seq")
    return jax.shard_map(body, mesh=mesh, in_specs=in_specs, out_specs=out_specs, check_vma=False)
```

profile of v0, /device:TPU:0, one launch (start us, length us, event | category | flops | bytes accessed | tf_op | source)
XLA Modules:
  0.0 235.4 jit_solution(12560561197507895507)
XLA Ops:
  6.5 0.0 copy-start
  6.5 0.0 all-gather.7.cloned.1.call-start
  6.5 1.6 copy.152
  8.2 0.0 all-gather.7.cloned.1.call-update
  8.2 0.9 fusion.14
  9.2 0.9 fusion.16
  10.1 0.0 copy-done
  10.1 0.8 fusion.34
  11.0 0.1 dynamic-slice_bitcast_fusion
  11.1 0.1 copy.171
  11.2 0.1 copy.172
  11.4 0.8 select_reduce_fusion.5
  12.2 0.8 select_reduce_fusion.4
  12.9 0.1 compare_bitcast_fusion
  13.0 0.1 copy.161
  13.1 0.7 add_compare_fusion
  13.8 1.0 select_reduce_fusion.1
  14.9 4.6 %reduce-window.6 = f32[4,24,4,128]{3,1,2,0:T(8,128)S(1)} reduce-window(f32[4,24,4,128]{3,1,2,0:T(8,128)S(1)} %bitcast.84, f32[]{:T(128)} %constant.8.clone.1), window={size=1x1x1x128 pad=0_0x0_0x0_0x127_0}, to_apply=%region_3.4 | reduce-window | flops 6242304 | bytes 393220 | tf_op jit(solution)/shard_map/reduce-window
  19.5 0.2 slice_reduce_fusion
  19.8 0.1 copy.162
  19.9 8.8 %copy.158 = bf16[4,512,1536]{1,2,0:T(8,128)(2,1)} copy(bf16[4,512,1536]{2,1,0:T(8,128)(2,1)} %param.16) | data formatting | bytes 12582912 | tf_op args[5]
  28.7 0.0 copy-start.1
  28.7 8.7 %copy.163 = bf16[4,512,1536]{1,2,0:T(8,128)(2,1)} copy(bf16[4,512,1536]{2,1,0:T(8,128)(2,1)} %param.17) | data formatting | bytes 12582912 | tf_op args[6]
  37.4 30.2 %all-gather.4 = f32[8,4,24]{2,1,0:T(4,128)S(1)} all-gather(f32[1,4,24]{2,1,0:T(4,128)S(1)} %bitcast.88), channel_id=2, replica_groups=mesh['fsdp'=16,'seq'=8] {'seq'}, dimensions={0}, use_global_device_ids=true | all-gather | bytes 3456 | tf_op jit(solution)/shard_map/all_gather | solution.py:73
  67.6 0.1 select_reduce_fusion.3
  67.7 0.0 copy-done.1
  67.8 0.1 fusion.13
  67.9 0.0 all-gather.7.cloned.1.call-done
  67.9 2.4 %fusion.4 = bf16[20,3,3,64]{3,0,2,1:T(8,128)(2,1)S(1)} fusion(bf16[1536,3,3,64]{0,2,1,3:T(4,128)(2,1)} %all-gather.7.cloned.1.call-done, bf16[20,1536,1,1]{1,0,2,3:T(8,128)(2,1)S(1)} %reshape.189), kind=kOutput, calls=%fused_computation.7 | convolution fusion | flops 35400960 | bytes 1853952 | tf_op jit(solution)/shard_map/nd,dchk->nchk/dot_general | solution.py:54
  70.4 0.2 copy.188
  70.6 0.1 fusion.21
  70.8 0.2 copy.170
  70.9 0.2 select_reduce_fusion.2
  71.1 0.1 copy.177
  71.2 0.1 copy.174
  71.3 38.0 %all_gather.19 = bf16[20,3,1536]{0,1,2:T(4,128)(2,1)S(1)} all-gather(bf16[20,3,192]{0,1,2:T(4,128)(2,1)S(1)} %bitcast.83), channel_id=1, replica_groups=mesh['fsdp'=16,'seq'=8] {'seq'}, dimensions={2}, use_global_device_ids=true | all-gather | bytes 207360 | tf_op jit(solution)/shard_map/all_gather | solution.py:61
  109.3 0.9 copy.156
  110.2 0.2 reshape.177
  110.5 3.9 %select_reduce_fusion = (f32[4,24,5]{2,1,0:T(8,128)S(1)}, f32[4,24,5,512]{3,2,1,0:T(8,128)S(1)}) fusion(pred[4,512]{1,0:T(4,128)(4,1)S(1)} %add_compare_fusion, f32[4,24,5]{2,1,0:T(8,128)S(1)} %copy.162, f32[4,24,512]{2,1,0:T(8,128)S(1)} %fusion.13, bf16[4,512,24,64]{1,3,2,0:T(8,128)(2,1)} %bitcast.78, bf16[4,5,1,24,64]{4,3,1,0,2:T(8,128)(2,1)S(1)} %slice.24), kind=kOutput, calls=%fused_computation.3 | convolution fusion | flops 32685600 | bytes 7538432 | tf_op jit(solution)/shard_map/rmhd,rthd->rhmt/dot_general | solution.py:81
  114.3 0.1 copy.165
  114.4 0.5 fusion.2
  114.9 0.1 copy.182
  115.0 34.2 %all-gather.3 = f32[32,24,5]{1,2,0:T(8,128)S(1)} all-gather(f32[4,24,5]{1,2,0:T(8,128)S(1)} %copy.182), channel_id=5, replica_groups=mesh['fsdp'=16,'seq'=8] {'seq'}, dimensions={0}, use_global_device_ids=true | all-gather | bytes 17280 | tf_op jit(solution)/shard_map/all_gather | solution.py:97
  149.2 34.2 %all-gather.2 = f32[32,24,5]{1,2,0:T(8,128)S(1)} all-gather(f32[4,24,5]{1,2,0:T(8,128)S(1)} %copy.165), channel_id=4, replica_groups=mesh['fsdp'=16,'seq'=8] {'seq'}, dimensions={0}, use_global_device_ids=true | all-gather | bytes 17280 | tf_op jit(solution)/shard_map/all_gather | solution.py:96
  183.4 0.1 dynamic-slice_reduce_fusion
  183.6 0.1 copy.176
  183.7 0.1 multiply_reduce_fusion.1
  183.8 0.1 copy.178
  183.9 0.2 fusion.37
  184.1 0.1 copy.184
  184.3 0.1 copy.175
  184.4 0.1 copy.185
  184.5 4.6 %fusion.8 = f32[4,24,5,64]{3,2,1,0:T(8,128)S(1)} fusion(bf16[4,512,24,64]{1,3,2,0:T(8,128)(2,1)} %bitcast.79, f32[4,24,5,512]{3,2,1,0:T(8,128)S(1)} %get-tuple-element.19, f32[4,24,5]{2,1,0:T(8,128)S(1)} %get-tuple-element.18, pred[4,512]{1,0:T(4,128)(4,1)S(1)} %add_compare_fusion), kind=kOutput, calls=%fused_computation.10 | convolution fusion | flops 32194560 | bytes 7401344 | tf_op jit(solution)/shard_map/rhmt,rthd->rhmd/dot_general | solution.py:89
  189.1 0.1 copy.164
  189.1 38.2 %all-gather.1 = f32[32,24,5,64]{3,1,2,0:T(8,128)S(1)} all-gather(f32[4,24,5,64]{3,1,2,0:T(8,128)S(1)} %copy.164), channel_id=3, replica_groups=mesh['fsdp'=16,'seq'=8] {'seq'}, dimensions={0}, use_global_device_ids=true | all-gather | bytes 1105920 | tf_op jit(solution)/shard_map/all_gather | solution.py:98
  227.4 0.3 multiply_reduce_fusion
  227.6 0.1 fusion.20
  227.8 0.1 select_convert_fusion
  227.9 0.7 convert_element_type.27
  (17 shorter events, 0.3 us)
Async XLA Ops:
  6.5 3.6 %copy-start = (bf16[1536,24]{0,1:T(8,128)(2,1)S(1)}, bf16[1536,24]{0,1:T(8,128)(2,1)}, u32[]{:S(2)}) copy-start(bf16[1536,24]{0,1:T(8,128)(2,1)} %param.14) | copy-start | bytes 221188
  6.5 61.4 %all-gather.7.cloned.1.call-start = ((), (), s32[]{:S(2)}) async-start(), calls=%async_computation | async-start | bytes 2506752 | tf_op jit(solution)/shard_map/all_gather | solution.py:57
  28.7 39.0 %copy-start.1 = (s32[4]{0:T(128)S(1)}, s32[4]{0:T(128)}, u32[]{:S(2)}) copy-start(s32[4]{0:T(128)} %param.21) | copy-start | bytes 52
Sparse Core Ops, SparseCore 0:
  9.1 37.0 all-gather.6
where the time goes:
time: 236 us; the launch traced here: 235 us
  blocking collectives  175 us (74%)
  local copies, waits for them, and re-layouts  23.3 us (10%)
  between operations  13.6 us (6%)
  matrix products  12 us (5%)
  other arithmetic  11.7 us (5%)
    all_gather x1, blocking collectives, body(): lax.all_gather(accum[None], 'seq', axis=0, tiled=True)  38.2 us
    all_gather x1, blocking collectives, body(): lax.all_gather(own_part, 'seq', axis=2, tiled=True)  38 us
    all_gather x1, blocking collectives, body(): lax.all_gather(row_max[None], 'seq', axis=0, tiled=True)  34.2 us
    all_gather x1, blocking collectives, body(): lax.all_gather(weight_sum[None], 'seq', axis=0, tiled=True)  34.2 us
    all_gather x1, blocking collectives, body(): all_totals = lax.all_gather(piece_total[None], 'seq', axis=0, tiled=True)  30.2 us
    unnamed x7, local copies, waits for them, and re-layouts  19.1 us
  transfers between devices with their start and end apart: 1, of which 0 were waited for; matrix products, arithmetic and copies ran while one was open for 12% of the time, Pallas kernels for 0%

commit v1 on v0

--- a/solution.py
+++ b/solution.py
@@ -70,7 +70,9 @@
     live_mask = positions < cache_lengths[:, None]
     masked = jnp.where(live_mask[:, None, :], cache_forget, 0.0)
     piece_total = jnp.sum(masked, axis=-1)
-    all_totals = lax.all_gather(piece_total[None], "seq", axis=0, tiled=True)
+    all_totals = jnp.concatenate(
+        lax.all_to_all(jnp.stack([piece_total[None]] * lax.axis_size("seq")), "seq", 0, 0), axis=0
+    )
     later_piece = (piece_of_slot.T > own_piece[None, :])[:, :, None]
     later_sum = jnp.sum(jnp.where(later_piece, all_totals, 0.0), axis=0)
     trailing_part = piece_total[..., None] - jnp.cumsum(masked, axis=-1) + later_sum[..., None]

time: 236 us -> 214 us (0.907)
  blocking collectives: 175 us -> 144 us
  starting transfers between devices: 0.01 us -> 7.05 us
  waiting for transfers between devices: 0.04 us -> 3.93 us
    all_gather x1 -> x0, blocking collectives: 30.2 us -> none  [body(): all_totals = lax.all_gather(piece_total[None], 'seq', axis=0, tiled=True)]
    all_to_all x0 -> x1, starting transfers between devices: none -> 7.01 us  [body(): lax.all_to_all(jnp.stack([piece_total[None]] * lax.axis_size('seq')), 'se...]
    all_gather x1, waiting for transfers between devices: 0.02 us -> 3.91 us  [body(): lax.all_gather(w_qkv, 'fsdp', axis=3, tiled=True)]
    unnamed x7 -> x15, local copies, waits for them, and re-layouts: 19.1 us -> 19.1 us
  transfers between devices with their start and end apart: 1 -> 2, of which waited for: 0 -> 1; matrix products, arithmetic and copies ran while one was open for 12% -> 13% of each run, Pallas kernels for 0% -> 0%
where the time goes in v1:
time: 214 us; the launch traced here: 213 us
  blocking collectives  144 us (67%)
  local copies, waits for them, and re-layouts  23.8 us (11%)
  between operations  13.6 us (6%)
  matrix products  11.3 us (5%)
  other arithmetic  9.36 us (4%)
  starting transfers between devices  7.05 us (3%)
  waiting for transfers between devices  3.93 us (2%)
    all_gather x1, blocking collectives, body(): lax.all_gather(accum[None], 'seq', axis=0, tiled=True)  38.2 us
    all_gather x1, blocking collectives, body(): lax.all_gather(own_part, 'seq', axis=2, tiled=True)  37.7 us
    all_gather x1, blocking collectives, body(): lax.all_gather(weight_sum[None], 'seq', axis=0, tiled=True)  34.2 us
    all_gather x1, blocking collectives, body(): lax.all_gather(row_max[None], 'seq', axis=0, tiled=True)  34.2 us
    unnamed x15, local copies, waits for them, and re-layouts  19.1 us
    all_to_all x1, starting transfers between devices, body(): lax.all_to_all(jnp.stack([piece_total[None]] * lax.axis_size('seq')), 'se...  7.01 us
    another operation x2, other arithmetic  4.64 us
    dot_general x1, matrix products, body(): jnp.einsum('rhmt,rthd->rhmd', attn_weights.astype(jnp.bfloat16), value_ro...  4.57 us
  transfers between devices with their start and end apart: 2, of which 1 were waited for; matrix products, arithmetic and copies ran while one was open for 13% of the time, Pallas kernels for 0%

profile of v1, /device:TPU:0, one launch (start us, length us, event | category | flops | bytes accessed | tf_op | source)
XLA Modules:
  0.0 213.4 jit_solution(2983240989300911069)
XLA Ops:
  6.5 0.0 copy-start
  6.5 0.0 copy-start.5
  6.6 0.0 all-gather.5.cloned.1.call-start
  6.6 1.7 copy.154
  8.3 0.0 all-gather.5.cloned.1.call-update
  8.3 0.8 select_reduce_fusion.4
  9.1 0.7 add_compare_fusion
  9.8 1.0 select_reduce_fusion.1
  10.9 0.6 stack.3
  11.5 7.0 %all-to-all-start = ((f32[8,1,4,24]{3,2,1,0:T(4,128)}), f32[8,1,4,24]{3,2,1,0:T(4,128)S(1)}, u32[]{:S(2)}, u32[]{:S(2)}) async-start(f32[8,1,4,24]{3,2,1,0:T(4,128)} %stack.3), calls=%async_computation | async-start | bytes 32768 | tf_op jit(solution)/shard_map/all_to_all | solution.py:74
  18.5 4.6 %reduce-window.6 = f32[4,24,4,128]{3,1,2,0:T(8,128)S(1)} reduce-window(f32[4,24,4,128]{3,1,2,0:T(8,128)S(1)} %bitcast.87, f32[]{:T(128)} %constant.8.clone.1), window={size=1x1x1x128 pad=0_0x0_0x0_0x127_0}, to_apply=%region_3.4 | reduce-window | flops 6242304 | bytes 393220 | tf_op jit(solution)/shard_map/reduce-window
  23.1 0.0 copy-done.1
  23.1 0.1 fusion.14
  23.2 0.0 copy-done.2
  23.2 0.1 fusion.16
  23.3 0.0 copy-done
  23.4 0.0 copy-done.4
  23.4 0.2 fusion.35
  23.6 0.1 dynamic-slice_bitcast_fusion
  23.7 0.0 copy-done.3
  23.7 0.1 select_reduce_fusion.3
  23.8 0.2 slice_reduce_fusion
  24.0 0.1 compare_bitcast_fusion
  24.1 0.1 copy.173
  24.3 0.1 copy.174
  24.4 0.1 copy.163
  24.5 0.1 copy.164
  24.6 8.7 %copy.160 = bf16[4,512,1536]{1,2,0:T(8,128)(2,1)} copy(bf16[4,512,1536]{2,1,0:T(8,128)(2,1)} %param.16) | data formatting | bytes 12582912 | tf_op args[5]
  33.4 8.7 %copy.165 = bf16[4,512,1536]{1,2,0:T(8,128)(2,1)} copy(bf16[4,512,1536]{2,1,0:T(8,128)(2,1)} %param.17) | data formatting | bytes 12582912 | tf_op args[6]
  42.0 0.0 all-to-all-done
  42.1 0.1 fusion.24
  42.1 0.1 fusion.13
  42.3 3.9 %all-gather.5.cloned.1.call-done = bf16[1536,3,3,64]{0,2,1,3:T(4,128)(2,1)} async-done(((bf16[1536,3,3,4]{0,2,1,3:T(4,128)(2,1)}), bf16[1536,3,3,64]{0,2,1,3:T(4,128)(2,1)}) %all-gather.5.cloned.1.call-update) | async-done | bytes 1769488 | tf_op jit(solution)/shard_map/all_gather | solution.py:57
  46.2 2.4 %fusion.4 = bf16[20,3,3,64]{3,0,2,1:T(8,128)(2,1)S(1)} fusion(bf16[1536,3,3,64]{0,2,1,3:T(4,128)(2,1)} %all-gather.5.cloned.1.call-done, bf16[20,1536,1,1]{1,0,2,3:T(8,128)(2,1)S(1)} %reshape.191), kind=kOutput, calls=%fused_computation.7 | convolution fusion | flops 35400960 | bytes 1853952 | tf_op jit(solution)/shard_map/nd,dchk->nchk/dot_general | solution.py:54
  48.6 0.2 copy.190
  48.9 0.1 fusion.21
  49.0 0.2 copy.172
  49.2 0.2 select_reduce_fusion.2
  49.4 0.1 copy.179
  49.5 0.1 copy.176
  49.6 37.7 %all_gather.16 = bf16[20,3,1536]{0,1,2:T(4,128)(2,1)S(1)} all-gather(bf16[20,3,192]{0,1,2:T(4,128)(2,1)S(1)} %bitcast.86), channel_id=1, replica_groups=mesh['fsdp'=16,'seq'=8] {'seq'}, dimensions={2}, use_global_device_ids=true | all-gather | bytes 207360 | tf_op jit(solution)/shard_map/all_gather | solution.py:61
  87.3 0.9 copy.158
  88.2 0.2 reshape.182
  88.5 3.9 %select_reduce_fusion = (f32[4,24,5]{2,1,0:T(8,128)S(1)}, f32[4,24,5,512]{3,2,1,0:T(8,128)S(1)}) fusion(pred[4,512]{1,0:T(4,128)(4,1)S(1)} %add_compare_fusion, f32[4,24,5]{2,1,0:T(8,128)S(1)} %copy.164, f32[4,24,512]{2,1,0:T(8,128)S(1)} %fusion.13, bf16[4,512,24,64]{1,3,2,0:T(8,128)(2,1)} %bitcast.81, bf16[4,5,1,24,64]{4,3,1,0,2:T(8,128)(2,1)S(1)} %slice.24), kind=kOutput, calls=%fused_computation.3 | convolution fusion | flops 32685600 | bytes 7538432 | tf_op jit(solution)/shard_map/rmhd,rthd->rhmt/dot_general | solution.py:83
  92.3 0.1 copy.167
  92.4 0.5 fusion.2
  92.9 0.1 copy.184
  93.0 34.2 %all-gather.2 = f32[32,24,5]{1,2,0:T(8,128)S(1)} all-gather(f32[4,24,5]{1,2,0:T(8,128)S(1)} %copy.184), channel_id=4, replica_groups=mesh['fsdp'=16,'seq'=8] {'seq'}, dimensions={0}, use_global_device_ids=true | all-gather | bytes 17280 | tf_op jit(solution)/shard_map/all_gather | solution.py:99
  127.2 34.2 %all-gather.1 = f32[32,24,5]{1,2,0:T(8,128)S(1)} all-gather(f32[4,24,5]{1,2,0:T(8,128)S(1)} %copy.167), channel_id=3, replica_groups=mesh['fsdp'=16,'seq'=8] {'seq'}, dimensions={0}, use_global_device_ids=true | all-gather | bytes 17280 | tf_op jit(solution)/shard_map/all_gather | solution.py:98
  161.4 0.1 dynamic-slice_reduce_fusion
  161.5 0.1 copy.178
  161.6 0.1 multiply_reduce_fusion.1
  161.8 0.1 copy.180
  161.9 0.2 fusion.38
  162.1 0.1 copy.186
  162.2 0.1 copy.177
  162.3 0.1 copy.187
  162.5 4.6 %fusion.8 = f32[4,24,5,64]{3,2,1,0:T(8,128)S(1)} fusion(bf16[4,512,24,64]{1,3,2,0:T(8,128)(2,1)} %bitcast.82, f32[4,24,5,512]{3,2,1,0:T(8,128)S(1)} %get-tuple-element.19, f32[4,24,5]{2,1,0:T(8,128)S(1)} %get-tuple-element.18, pred[4,512]{1,0:T(4,128)(4,1)S(1)} %add_compare_fusion), kind=kOutput, calls=%fused_computation.10 | convolution fusion | flops 32194560 | bytes 7401344 | tf_op jit(solution)/shard_map/rhmt,rthd->rhmd/dot_general | solution.py:91
  167.0 0.1 copy.166
  167.1 38.2 %all-gather = f32[32,24,5,64]{3,1,2,0:T(8,128)S(1)} all-gather(f32[4,24,5,64]{3,1,2,0:T(8,128)S(1)} %copy.166), channel_id=2, replica_groups=mesh['fsdp'=16,'seq'=8] {'seq'}, dimensions={0}, use_global_device_ids=true | all-gather | bytes 1105920 | tf_op jit(solution)/shard_map/all_gather | solution.py:100
  205.3 0.3 multiply_reduce_fusion
  205.6 0.1 fusion.20
  205.7 0.1 select_convert_fusion
  205.8 0.7 convert_element_type.27
  (22 shorter events, 0.3 us)
Async XLA Ops:
  6.5 16.8 %copy-start = (bf16[1536,24]{0,1:T(8,128)(2,1)S(1)}, bf16[1536,24]{0,1:T(8,128)(2,1)}, u32[]{:S(2)}) copy-start(bf16[1536,24]{0,1:T(8,128)(2,1)} %param.14) | copy-start | bytes 221188
  6.5 17.1 %copy-start.3 = (s32[4,8]{1,0:T(4,128)S(1)}, s32[4,8]{1,0:T(4,128)}, u32[]{:S(2)}) copy-start(s32[4,8]{1,0:T(4,128)} %param.20) | copy-start | bytes 388
  6.5 16.6 %copy-start.1 = (bf16[4,5,1536]{2,0,1:T(4,128)(2,1)S(1)}, bf16[4,5,1536]{2,0,1:T(4,128)(2,1)}, u32[]{:S(2)}) copy-start(bf16[4,5,1536]{2,0,1:T(4,128)(2,1)} %param.11) | copy-start | bytes 184324
  6.5 16.7 %copy-start.2 = (f32[1536]{0:T(1024)S(1)}, f32[1536]{0:T(1024)}, u32[]{:S(2)}) copy-start(f32[1536]{0:T(1024)} %param.12) | copy-start | bytes 18436
  6.5 16.8 %copy-start.4 = (f32[24]{0:T(128)S(1)}, f32[24]{0:T(128)}, u32[]{:S(2)}) copy-start(f32[24]{0:T(128)} %param.15) | copy-start | bytes 292
  6.5 17.4 %copy-start.5 = (s32[4]{0:T(128)S(1)}, s32[4]{0:T(128)}, u32[]{:S(2)}) copy-start(s32[4]{0:T(128)} %param.21) | copy-start | bytes 52
  6.6 39.6 %all-gather.5.cloned.1.call-start = ((), (), s32[]{:S(2)}) async-start(), calls=%async_computation.1 | async-start | bytes 2506752 | tf_op jit(solution)/shard_map/all_gather | solution.py:57
  11.5 30.6 %all-to-all-start = ((f32[8,1,4,24]{3,2,1,0:T(4,128)}), f32[8,1,4,24]{3,2,1,0:T(4,128)S(1)}, u32[]{:S(2)}, u32[]{:S(2)}) async-start(f32[8,1,4,24]{3,2,1,0:T(4,128)} %stack.3), calls=%async_computation | async-start | bytes 32768 | tf_op jit(solution)/shard_map/all_to_all | solution.py:74
Sparse Core Ops, SparseCore 0:
  9.1 37.0 all-gather.4
